TPU v7x, 256 devices: a whole 4x4x8 slice. The times are simulated.
256 devices in a mesh: ctx: 32 (over x, z), head: 8 (over y, core).
Axes of the slice: x: 4, y: 4, z: 8, core: 2. Of those that a mesh axis runs over, the one named last changes fastest.
Arguments:
- features: bfloat16 [8192, 16384], P('ctx', 'head'), may hold values from -6 to 6
- log_decay: float32 [256, 8192], P('head', 'ctx'), may hold values from -2 to 0, as said below
- step_size: float32 [256, 8192], P('head', 'ctx'), may hold values from 0.0002 to 0.002
- b_matrix: bfloat16 [8192, 2048], P('ctx', 'head'), may hold values from -6 to 6
- c_matrix: bfloat16 [8192, 2048], P('ctx', 'head'), may hold values from -6 to 6
- skip_gain: float32 [256], P('head'), may hold values from 0.5 to 1.5
Outputs:
- mixed: bfloat16 [8192, 16384], P('ctx', 'head')
Inputs may be any that keep to these rules, and one draw needn't show every extreme that they name: `log_decay`: every entry is negative.
All inputs are finite; a program needn't handle non-finite values.
Results may differ from a plain program's by a relative error of at most 0.0013.
Values sent between devices are 32-bit elements; how exact they have to be, the bound alone decides.
No kernel may reach another device: no remote copies, remote signals or barrier semaphores. Data moves between devices by JAX's collectives and lax.ppermute only.
A program may use at most 320 MiB of HBM per device.

v0:
```python
import jax
import jax.numpy as jnp
from jax import lax
from jax.sharding import PartitionSpec as P

N = 256
SPAN = 128


def carried_in(x, axis, combine, identity, reverse):
    length, place = (lax.axis_size(axis), lax.axis_index(axis))
    everything = jax.tree.map(lambda part: lax.all_gather(part, axis), x)
    start = jax.tree.map(
        lambda part, zero: jnp.broadcast_to(jnp.asarray(zero, part.dtype), part.shape), x, identity
    )

    def step(k, before):
        at = length - 1 - k if reverse else k
        reached = at > place if reverse else at < place
        new = combine(before, jax.tree.map(lambda part: part[at], everything))
        return jax.tree.map(lambda a, b: jnp.where(reached, a, b), new, before)

    return lax.fori_loop(0, length, step, start)


def from_root(block, axis, source):
    block = jnp.where(lax.axis_index(axis) == source, block, jnp.zeros_like(block))
    return lax.psum(block, axis)


def chain(earlier, later_pair):
    return (
        earlier[0] + later_pair[0],
        jnp.exp(later_pair[0])[:, None, None] * earlier[1] + later_pair[1],
    )


def on_device(features, log_decay, step_size, b_matrix, c_matrix, skip_gain):
    head_count = log_decay.shape[0]
    tok_rows = features.shape[0]
    head_width = features.shape[1] // head_count
    state_size = N
    group_count = b_matrix.shape[1] // state_size
    per_group = head_count // group_count
    span_count = tok_rows // SPAN
    half_count = span_count // 2
    cumulative = jnp.cumsum(log_decay.reshape(head_count, span_count, SPAN), axis=2)
    step_rows = step_size.reshape(head_count, span_count, SPAN)
    inputs = features.reshape(span_count, SPAN, head_count, head_width)
    grouped_inputs = features.reshape(span_count, SPAN, group_count, per_group, head_width)
    b_spans = b_matrix.reshape(span_count, SPAN, group_count, state_size)
    c_spans = c_matrix.reshape(span_count, SPAN, group_count, state_size)
    scores = jnp.einsum("ktgn,ksgn->gkts", c_spans, b_spans, preferred_element_type=jnp.float32)
    causal = jnp.arange(SPAN)[:, None] >= jnp.arange(SPAN)[None, :]
    cum_grouped = cumulative.reshape(group_count, per_group, span_count, SPAN)
    step_grouped = step_rows.reshape(group_count, per_group, span_count, SPAN)
    decay_gaps = jnp.where(causal, cum_grouped[..., :, None] - cum_grouped[..., None, :], -jnp.inf)
    weights = (scores[:, None] * jnp.exp(decay_gaps) * step_grouped[:, :, :, None, :]).astype(
        jnp.bfloat16
    )
    diagonal_part = jnp.einsum(
        "gqkts,ksgqp->ktgqp", weights, grouped_inputs, preferred_element_type=jnp.float32
    )
    diagonal_part = diagonal_part.reshape(span_count, SPAN, head_count, head_width)
    span_ends = cumulative[:, :, -1]
    coeffs = jnp.exp(span_ends[:, :, None] - cumulative) * step_rows
    weighted = (inputs * jnp.transpose(coeffs, (1, 2, 0))[:, :, :, None]).astype(jnp.bfloat16)
    weighted = weighted.reshape(span_count, SPAN, group_count, per_group, head_width)
    span_states = jnp.einsum(
        "ksgn,ksgqp->kgqpn", b_spans, weighted, preferred_element_type=jnp.float32
    )
    span_states = span_states.reshape(span_count, head_count, head_width, state_size)
    totals = jnp.transpose(span_ends).reshape(2, half_count, head_count)
    grouped = span_states.reshape(2, half_count, head_count, head_width, state_size)

    def advance(running, element):
        return (jnp.exp(element[0])[:, :, None, None] * running + element[1], running)

    start = jnp.zeros((2, head_count, head_width, state_size), jnp.float32)
    block_states, prefix = lax.scan(
        advance, start, (jnp.swapaxes(totals, 0, 1), jnp.swapaxes(grouped, 0, 1))
    )
    shifted = jnp.concatenate([jnp.zeros((2, 1, head_count), jnp.float32), totals[:, :-1]], axis=1)
    before = jnp.cumsum(shifted, axis=1)
    block_decay = jnp.sum(totals, axis=1)
    front_pair = (block_decay[0], block_states[0])
    back_pair = (block_decay[1], block_states[1])
    neutral = (
        jnp.zeros((head_count,), jnp.float32),
        jnp.zeros((head_count, head_width, state_size), jnp.float32),
    )
    enter_front = carried_in(front_pair, "ctx", chain, neutral, False)
    through_front = chain(enter_front, front_pair)[1]
    middle = from_root(through_front, "ctx", lax.axis_size("ctx") - 1)
    behind = carried_in(back_pair, "ctx", chain, neutral, True)
    enter_back = jnp.exp(behind[0])[:, None, None] * middle + behind[1]
    entering = jnp.stack([enter_front[1], enter_back])
    span_enter = jnp.exp(before)[:, :, :, None, None] * entering[:, None] + jnp.swapaxes(
        prefix, 0, 1
    )
    state_bf = span_enter.astype(jnp.bfloat16)
    state_part = jnp.einsum(
        "ktgn,kgqpn->ktgqp", c_spans, state_bf, preferred_element_type=jnp.float32
    )
    state_part = state_part.reshape(span_count, SPAN, head_count, head_width)
    state_part = state_part * jnp.transpose(jnp.exp(cumulative), (1, 2, 0))[:, :, :, None]
    output_rows = (
        diagonal_part + state_part + skip_gain[None, None, :, None] * inputs.astype(jnp.float32)
    )
    return output_rows.reshape(tok_rows, head_count * head_width).astype(jnp.bfloat16)


def solution(mesh):
    placed = (
        P("ctx", "head"),
        P("head", "ctx"),
        P("head", "ctx"),
        P("ctx", "head"),
        P("ctx", "head"),
        P("head"),
    )
    return jax.shard_map(
        on_device, mesh=mesh, in_specs=placed, out_specs=P("ctx", "head"), check_vma=False
    )
```

profile of v0, /device:TPU:8, one launch (start us, length us, event | category | flops | bytes accessed | tf_op | source)
XLA Modules:
  0.0 1049.9 jit_solution(3869095595849692370)
XLA Ops:
  23.7 43.5 %all-gather = f32[32,1,32]{2,1,0:T(1,128)S(1)} all-gather(f32[1,1,32]{2,1,0:T(1,128)S(1)} %get-tuple-element.343), channel_id=1, replica_groups=mesh['ctx'=32,'head'=8] {'ctx'}, dimensions={0}, use_global_device_ids=true | all-gather | bytes 4224 | tf_op jit(solution)/shard_map/all_gather | solution.py:12
  67.2 38.4 %all-gather.1 = f32[32,1,32]{2,1,0:T(1,128)S(1)} all-gather(f32[1,1,32]{2,1,0:T(1,128)S(1)} %get-tuple-element.342), channel_id=1, replica_groups=mesh['ctx'=32,'head'=8] {'ctx'}, dimensions={0}, use_global_device_ids=true | all-gather | bytes 4224 | tf_op jit(solution)/shard_map/all_gather | solution.py:12
  105.6 344.3 %all-gather.5.cloned.1.call-done = f32[32,32,64,256]{3,2,1,0:T(8,128)} async-done(((f32[1,32,64,256]{3,2,1,0:T(8,128)}), f32[32,32,64,256]{3,2,1,0:T(8,128)}) %all-gather.5.cloned.1.call-update) | async-done | bytes 67108880 | tf_op jit(solution)/shard_map/all_gather | solution.py:12
  449.9 127.7 %while.37 = (s32[]{:T(128)}, f32[32,64,256]{2,1,0:T(8,128)}, s32[]{:T(128)}, f32[32,32]{1,0:T(8,128)S(1)}, f32[32,32,64,256]{3,2,1,0:T(8,128)}, /*index=5*/s32[]{:T(128)}, s32[]{:T(128)}) while((s32[]{:T(128)}, f32[32,64,256]{2,1,0:T(8,128)}, s32[]{:T(128)}, f32[32,32]{1,0:T(8,128)S(1)}, f32[32,32,64,256]{3,2,1,0:T(8,128)}, ...), condition=%wide.region_2.3_spmd.clone, body=%wide.region_1.2_spmd.clone.sunk | while | flops 2097156 | bytes 6291945 | solution.py:23
  457.1 3.9 fusion.37
  461.0 4.6 fusion.37
  465.6 4.3 fusion.37
  473.8 3.9 fusion.37
  477.8 4.0 fusion.37
  481.7 3.9 fusion.37
  485.7 3.9 fusion.37
  489.6 3.9 fusion.37
  493.5 3.9 fusion.37
  497.4 4.0 fusion.37
  501.4 3.9 fusion.37
  505.4 3.9 fusion.37
  509.3 3.9 fusion.37
  513.2 3.9 fusion.37
  517.1 4.0 fusion.37
  521.1 3.9 fusion.37
  525.0 3.9 fusion.37
  528.9 3.9 fusion.37
  532.9 3.9 fusion.37
  536.7 3.9 fusion.37
  556.2 4.1 fusion.37
  560.3 5.1 fusion.37
  565.5 4.3 fusion.37
  573.6 4.0 fusion.37
  577.6 4.9 convert_bitcast_fusion
  582.5 298.2 %all-gather.7.cloned.1.call-done = f32[32,32,64,256]{3,2,1,0:T(8,128)} async-done(((f32[1,32,64,256]{3,2,1,0:T(8,128)}), f32[32,32,64,256]{3,2,1,0:T(8,128)}) %all-gather.7.cloned.1.call-update) | async-done | bytes 67108880 | tf_op jit(solution)/shard_map/all_gather | solution.py:12
  880.7 69.6 %while.38 = (s32[]{:T(128)}, f32[32]{0:T(128)S(1)}, f32[32,64,256]{2,1,0:T(8,128)S(1)}, s32[]{:T(128)}, f32[32,32]{1,0:T(8,128)S(1)}, /*index=5*/f32[32,32,64,25...) while((s32[]{:T(128)}, f32[32]{0:T(128)S(1)}, f32[32,64,256]{2,1,0:T(8,128)S(1)}, ...), condition=%wide.region_4.5_spmd.clone, body=%wide.region_3.4_spmd.clone.sunk | while | flops 2097256 | bytes 6292273 | solution.py:23
  950.3 85.2 %all-reduce.2.cloned.1.call-done = f32[32,64,256]{2,1,0:T(8,128)} async-done(((f32[32,64,256]{2,1,0:T(8,128)}), f32[32,64,256]{2,1,0:T(8,128)}) %all-reduce.2.cloned.1.call-update) | async-done | bytes 2097168 | tf_op jit(solution)/shard_map/psum | solution.py:28
  (156 shorter events, 124.0 us)
Async XLA Ops:
  6.5 5.3 copy-start
  6.5 443.4 %all-gather.5.cloned.1.call-start = ((), (), s32[]{:S(2)}) async-start(), calls=%async_computation | async-start | bytes 69206016 | tf_op jit(solution)/shard_map/all_gather | solution.py:12
  10.8 1.8 copy-start.3
  12.6 3.3 copy-start.1
  15.8 0.9 copy-start.6
  15.8 0.9 copy-start.5
  15.9 864.8 %all-gather.7.cloned.1.call-start = ((), (), s32[]{:S(2)}) async-start(), calls=%async_computation.1 | async-start | bytes 69206016 | tf_op jit(solution)/shard_map/all_gather | solution.py:12
  16.6 1018.8 %all-reduce.2.cloned.1.call-start = ((), (), s32[]{:S(2)}) async-start(), calls=%async_computation.2 | async-start | bytes 4194304 | tf_op jit(solution)/shard_map/psum | solution.py:28
  20.6 3.0 copy-start.7
  1035.5 2.0 copy-start.4
  1039.8 1.6 copy-start.2
Sparse Core Ops, SparseCore 0:
  16.0 433.8 all-gather.4
  452.5 428.1 all-gather.6
  884.2 151.2 all-reduce.1
where the time goes:
time: 1050 us
  waiting for transfers between devices  728 us (69%)
  other arithmetic  206 us (20%)
  blocking collectives  81.9 us (8%)
  local copies, waits for them, and re-layouts  14.1 us (1%)
  between operations  13.3 us (1%)
    all_gather x2, waiting for transfers between devices, carried_in(): everything = jax.tree.map(lambda part: lax.all_gather(part, axis), x)  642 us
    select_n x64, other arithmetic, step(): return jax.tree.map(lambda a, b: jnp.where(reached, a, b), new, before)  195 us
    psum x1, waiting for transfers between devices, from_root(): return lax.psum(block, axis)  85.2 us
    all_gather x2, blocking collectives, carried_in(): everything = jax.tree.map(lambda part: lax.all_gather(part, axis), x)  81.9 us
  transfers between devices with their start and end apart: 3, of which 3 were waited for; matrix products, arithmetic and copies ran while one was open for 20% of the time, Pallas kernels for 0%

commit v1 on v0

--- a/solution.py
+++ b/solution.py
@@ -25,7 +25,7 @@
 
 def from_root(block, axis, source):
     block = jnp.where(lax.axis_index(axis) == source, block, jnp.zeros_like(block))
-    return lax.psum(block, axis)
+    return jnp.sum(lax.all_gather(block, axis), axis=0)
 
 
 def chain(earlier, later_pair):

time: 1050 us -> 1350 us (1.29)
  waiting for transfers between devices: 728 us -> 1060 us
  other arithmetic: 206 us -> 170 us
    all_gather x0 -> x1, waiting for transfers between devices: none -> 360 us  [from_root(): return jnp.sum(lax.all_gather(block, axis), axis=0)]
    psum x1 -> x0, waiting for transfers between devices: 85.2 us -> none  [from_root(): return lax.psum(block, axis)]
    all_gather x2, waiting for transfers between devices: 642 us -> 701 us  [carried_in(): everything = jax.tree.map(lambda part: lax.all_gather(part, axis), x)]
    select_n x64, other arithmetic: 195 us -> 138 us  [step(): return jax.tree.map(lambda a, b: jnp.where(reached, a, b), new, before)]
    reduce_sum x0 -> x1, other arithmetic: none -> 22.2 us  [from_root(): return jnp.sum(lax.all_gather(block, axis), axis=0)]
  transfers between devices with their start and end apart: 3 -> 3, of which waited for: 3 -> 3; matrix products, arithmetic and copies ran while one was open for 20% -> 11% of each run, Pallas kernels for 0% -> 0%
where the time goes in v1:
time: 1350 us
  waiting for transfers between devices  1060 us (79%)
  other arithmetic  170 us (13%)
  blocking collectives  81.1 us (6%)
  local copies, waits for them, and re-layouts  15 us (1%)
    all_gather x2, waiting for transfers between devices, carried_in(): everything = jax.tree.map(lambda part: lax.all_gather(part, axis), x)  701 us
    all_gather x1, waiting for transfers between devices, from_root(): return jnp.sum(lax.all_gather(block, axis), axis=0)  360 us
    select_n x64, other arithmetic, step(): return jax.tree.map(lambda a, b: jnp.where(reached, a, b), new, before)  138 us
    all_gather x2, blocking collectives, carried_in(): everything = jax.tree.map(lambda part: lax.all_gather(part, axis), x)  81.1 us
  transfers between devices with their start and end apart: 3, of which 3 were waited for; matrix products, arithmetic and copies ran while one was open for 11% of the time, Pallas kernels for 0%

profile of v1, /device:TPU:8, one launch (start us, length us, event | category | flops | bytes accessed | tf_op | source)
XLA Modules:
  0.0 1348.0 jit_solution(5261642748415804444)
XLA Ops:
  12.6 2.5 fusion.26
  16.6 43.0 %all-gather.1 = f32[32,1,32]{2,1,0:T(1,128)S(1)} all-gather(f32[1,1,32]{2,1,0:T(1,128)S(1)} %get-tuple-element.343), channel_id=1, replica_groups=mesh['ctx'=32,'head'=8] {'ctx'}, dimensions={0}, use_global_device_ids=true | all-gather | bytes 4224 | tf_op jit(solution)/shard_map/all_gather | solution.py:12
  59.6 390.3 %all-gather.7.cloned.1.call-done = f32[32,32,64,256]{3,2,1,0:T(8,128)} async-done(((f32[1,32,64,256]{3,2,1,0:T(8,128)}), f32[32,32,64,256]{3,2,1,0:T(8,128)}) %all-gather.7.cloned.1.call-update) | async-done | bytes 67108880 | tf_op jit(solution)/shard_map/all_gather | solution.py:12
  449.9 70.4 %while.37 = (s32[]{:T(128)}, f32[32,64,256]{2,1,0:T(8,128)S(1)}, s32[]{:T(128)}, f32[32,32]{1,0:T(8,128)S(1)}, f32[32,32,64,256]{3,2,1,0:T(8,128)}, /*index=5*/s32[]{:T(128)}, s32[]{:T(128)}) while((s32[]{:T(128)}, f32[32,64,256]{2,1,0:T(8,128)S(1)}, s32[]{:T(128)}, f32[32,32]{1,0:T(8,128)S(1)}, f32[32,32,64,256]{3,2,1,0:T(8,128)}, ...), condition=%wide.region_2.3_spmd.clone, body=%wide.region_1.2_spmd.clone.sunk | while | flops 2097156 | bytes 6291945 | solution.py:23
  460.6 2.5 fusion.37
  463.1 2.4 fusion.37
  465.6 2.5 fusion.37
  472.4 2.2 fusion.37
  474.6 2.2 fusion.37
  492.0 2.2 fusion.37
  498.6 2.2 fusion.37
  500.8 2.2 fusion.37
  520.3 3.7 convert_bitcast_fusion
  525.1 3.6 fusion.20
  528.7 3.0 copy.27
  531.9 38.1 %all-gather.2 = f32[32,1,32]{2,1,0:T(1,128)S(1)} all-gather(f32[1,1,32]{2,1,0:T(1,128)S(1)} %get-tuple-element.342), channel_id=1, replica_groups=mesh['ctx'=32,'head'=8] {'ctx'}, dimensions={0}, use_global_device_ids=true | all-gather | bytes 4224 | tf_op jit(solution)/shard_map/all_gather | solution.py:12
  570.0 310.7 %all-gather.9.cloned.1.call-done = f32[32,32,64,256]{3,2,1,0:T(8,128)} async-done(((f32[1,32,64,256]{3,2,1,0:T(8,128)}), f32[32,32,64,256]{3,2,1,0:T(8,128)}) %all-gather.9.cloned.1.call-update) | async-done | bytes 67108880 | tf_op jit(solution)/shard_map/all_gather | solution.py:12
  880.6 70.8 %while.38 = (s32[]{:T(128)}, f32[32]{0:T(128)S(1)}, f32[32,64,256]{2,1,0:T(8,128)S(1)}, s32[]{:T(128)}, f32[32,32]{1,0:T(8,128)S(1)}, /*index=5*/f32[32,32,64,25...) while((s32[]{:T(128)}, f32[32]{0:T(128)S(1)}, f32[32,64,256]{2,1,0:T(8,128)S(1)}, ...), condition=%wide.region_4.5_spmd.clone, body=%wide.region_3.4_spmd.clone.sunk | while | flops 2097256 | bytes 6292273 | solution.py:23
  891.4 2.5 fusion.38
  893.9 2.4 fusion.38
  896.4 2.5 fusion.38
  903.3 2.2 fusion.38
  905.5 2.2 fusion.38
  907.7 2.1 fusion.38
  912.1 2.1 fusion.38
  914.3 2.1 fusion.38
  923.0 2.2 fusion.38
  925.2 2.2 fusion.38
  931.8 2.2 fusion.38
  934.0 2.1 fusion.38
  951.4 359.9 %all-gather.11.cloned.1.call-done = f32[1024,64,256]{2,1,0:T(8,128)} async-done(((f32[32,64,256]{2,1,0:T(8,128)}), f32[1024,64,256]{2,1,0:T(8,128)}) %all-gather.11.cloned.1.call-update) | async-done | bytes 67108880 | tf_op jit(solution)/shard_map/all_gather | solution.py:28
  1311.4 22.2 %reduce_sum.8 = f32[32,64,256]{2,1,0:T(8,128)} reduce(f32[32,32,64,256]{3,2,1,0:T(8,128)} %bitcast.16, f32[]{:T(128)} %constant.95.clone.1), dimensions={0}, to_apply=%region_5.6 | reduce | flops 16252928 | bytes 69206016 | tf_op jit(solution)/shard_map/reduce_sum | solution.py:28
  (157 shorter events, 110.7 us)
Async XLA Ops:
  6.5 5.3 copy-start
  6.5 443.3 %all-gather.7.cloned.1.call-start = ((), (), s32[]{:S(2)}) async-start(), calls=%async_computation | async-start | bytes 69206016 | tf_op jit(solution)/shard_map/all_gather | solution.py:12
  10.8 1.8 copy-start.3
  12.6 3.2 copy-start.1
  15.8 864.8 %all-gather.9.cloned.1.call-start = ((), (), s32[]{:S(2)}) async-start(), calls=%async_computation.1 | async-start | bytes 69206016 | tf_op jit(solution)/shard_map/all_gather | solution.py:12
  16.6 1294.8 %all-gather.11.cloned.1.call-start = ((), (), s32[]{:S(2)}) async-start(), calls=%async_computation.2 | async-start | bytes 69206016 | tf_op jit(solution)/shard_map/all_gather | solution.py:28
  524.0 0.8 copy-start.6
  524.0 0.9 copy-start.5
  528.7 3.0 copy-start.7
  1333.5 2.0 copy-start.4
  1337.9 1.6 copy-start.2
Sparse Core Ops, SparseCore 0:
  15.9 433.8 all-gather.6
  452.5 428.1 all-gather.8
  883.2 428.1 all-gather.10
